TPU v7x, 32 devices: a whole 2x2x4 slice. The times are simulated.
32 devices in a mesh: grp: 4 (over x, core), rel: 8 (over z, y).
Axes of the slice: x: 2, y: 2, z: 4, core: 2. Of those that a mesh axis runs over, the one named last changes fastest.
Arguments:
- head_ids: int32 [65536], P(('grp', 'rel')), may hold values from 0 to 1023
- relations: int32 [65536, 1], P(('grp', 'rel')), may hold values from 0 to 31; in each aligned block of 2048 rows (0 to 2047, 2048 to 4095, ...) at most 128 rows name the same one
- tail_ids: int32 [65536], P(('grp', 'rel')), may hold values from 0 to 1023
- neg_owner: int32 [1], replicated, may hold values from 0 to 31
- entities: bfloat16 [32768, 512], P(('grp', 'rel')), may hold values from -0.3984375 to 0.3984375
- rel_weight: float32 [32, 512, 512], P('rel'), may hold values from -6 to 6
- rel_accum: float32 [32, 512], P('rel'), may hold values from 0.001 to 0.1
Outputs:
- losses: bfloat16 [65536], P(('grp', 'rel'))
- head_grad: bfloat16 [65536, 512], P(('grp', 'rel'))
- new_rel: float32 [32, 512, 512], P('rel')
- new_accum: float32 [32, 512], P('rel')
Inputs may be any that keep to these rules, and one draw needn't show every extreme that they name: `head_ids`: a row of the device's own shard of 1024 entity rows. `tail_ids`: a row of the device's own shard of 1024 entity rows. `relations`: in the 2048 rows of one device no relation is named by more than 128 rows; some relation is named by exactly 128. `neg_owner`: a device index, counted grp first, then rel.
All inputs are finite; a program needn't handle non-finite values.
Results may differ from a plain program's by a relative error of at most 0.0095.
Values may be sent and summed in bfloat16 or wider, within the bound.
No kernel may reach another device: no remote copies, remote signals or barrier semaphores. Data moves between devices by JAX's collectives and lax.ppermute only.
A program may use at most 128 MiB of HBM per device.

v0:
```python
import jax
import jax.numpy as jnp
from jax import lax
from jax.sharding import PartitionSpec as P

LEARNING_RATE = 1.0
BF = jnp.bfloat16
F32 = jnp.float32


def broadcast(shard, axis, root):
    mine = lax.axis_index(axis) == root
    return lax.psum(jnp.where(mine, shard, jnp.zeros_like(shard)), axis)


def one_hot(ids, count):
    return (ids[:, None] == jnp.arange(count, dtype=jnp.int32)[None, :]).astype(BF)


def select_rows(selector, rows):
    return jnp.dot(selector, rows, preferred_element_type=F32).astype(BF)


def select_back(selector, rows):
    return lax.dot_general(
        selector, rows, (((0,), (0,)), ((), ())), preferred_element_type=F32
    ).astype(BF)


def score_rows(query_rows, tail_rows, negatives):
    positive = jnp.sum(query_rows.astype(F32) * tail_rows.astype(F32), axis=-1)
    neg_scores = lax.dot_general(
        query_rows, negatives, (((1,), (1,)), ((), ())), preferred_element_type=F32
    )
    losses = jax.nn.softplus(-positive) + jnp.mean(jax.nn.softplus(neg_scores), axis=-1)
    coefs = (jax.nn.sigmoid(neg_scores) / negatives.shape[0]).astype(BF)
    grad_query = -jax.nn.sigmoid(-positive)[:, None] * tail_rows.astype(F32)
    grad_query = grad_query + jnp.dot(coefs, negatives, preferred_element_type=F32)
    return (losses.astype(BF), grad_query.astype(BF))


def adagrad(weight, accumulator, gradient):
    new_accum = accumulator + jnp.mean(gradient * gradient, axis=-1)
    return (weight - LEARNING_RATE * gradient / jnp.sqrt(new_accum)[..., None], new_accum)


def broadcast_rows(shard, axis, root):
    mine = lax.axis_index(axis) == root
    return lax.psum(jnp.where(mine, shard, jnp.zeros_like(shard)), axis)


def slot_ranks(rel_ids, bucket_count):
    one_hot = (rel_ids[..., None] == jnp.arange(bucket_count, dtype=jnp.int32)).astype(jnp.int32)
    running = jnp.cumsum(one_hot, axis=-2) - 1
    return jnp.sum(one_hot * running, axis=-1)


def score_rows_rows(query_rows, tail_rows, negatives):
    positive = jnp.sum(query_rows.astype(jnp.float32) * tail_rows.astype(jnp.float32), axis=-1)
    neg_scores = jnp.dot(query_rows, negatives.T, preferred_element_type=jnp.float32)
    losses = jax.nn.softplus(-positive) + jnp.mean(jax.nn.softplus(neg_scores), axis=-1)
    coefs = (jax.nn.sigmoid(neg_scores) / negatives.shape[0]).astype(jnp.bfloat16)
    grad_query = -jax.nn.sigmoid(-positive)[:, None] * tail_rows.astype(jnp.float32)
    grad_query = grad_query + jnp.dot(coefs, negatives, preferred_element_type=jnp.float32)
    return (losses.astype(jnp.bfloat16), grad_query.astype(jnp.bfloat16))


def adagrad_rows(weight, accumulator, gradient):
    new_accum = accumulator + jnp.mean(gradient * gradient, axis=-1)
    return (weight - LEARNING_RATE * gradient / jnp.sqrt(new_accum)[..., None], new_accum)


def to_buckets(values, position, layout):
    flat_shape = (layout[0] * layout[1] * layout[2],) + values.shape[1:]
    filled = jnp.zeros(flat_shape, values.dtype).at[position].set(values)
    return filled.reshape(layout + values.shape[1:])


def from_buckets(stacked, position):
    return stacked.reshape((-1,) + stacked.shape[3:])[position]


def per_device_rows(head_ids, relations, tail_ids, neg_owner, entities, rel_weight, rel_accum):
    rows_here = head_ids.shape[0]
    width = entities.shape[1]
    owner_count = lax.axis_size("rel")
    local_rels = rel_weight.shape[0]
    capacity = 2 * rows_here // (owner_count * local_rels)
    layout = (owner_count, local_rels, capacity)
    rel_ids = relations[:, 0]
    position = rel_ids * capacity + slot_ranks(rel_ids, owner_count * local_rels)
    head_rows = jnp.take(entities, head_ids, axis=0)
    tail_rows = jnp.take(entities, tail_ids, axis=0)
    matrices = rel_weight.astype(jnp.bfloat16)
    negatives = broadcast_rows(entities, ("grp", "rel"), neg_owner[0])
    held_rows, held_tails = (
        lax.all_to_all(
            to_buckets(head_rows, position, layout), "rel", split_axis=0, concat_axis=0, tiled=True
        ),
        lax.all_to_all(
            to_buckets(tail_rows, position, layout), "rel", split_axis=0, concat_axis=0, tiled=True
        ),
    )
    projected = jnp.einsum(
        "srcd,rde->srce", held_rows, matrices, preferred_element_type=jnp.float32
    ).astype(jnp.bfloat16)
    slot_losses, slot_grads = score_rows_rows(
        projected.reshape(-1, width), held_tails.reshape(-1, width), negatives
    )
    grad_rows = slot_grads.reshape(held_rows.shape)
    partial_value = jnp.einsum(
        "srcd,srce->rde", held_rows, grad_rows, preferred_element_type=jnp.float32
    )
    head_back = jnp.einsum(
        "srce,rde->srcd", grad_rows, matrices, preferred_element_type=jnp.float32
    ).astype(jnp.bfloat16)
    partial_value, head_back = (partial_value, head_back)
    back_grads, back_losses = (
        lax.all_to_all(head_back, "rel", split_axis=0, concat_axis=0, tiled=True),
        lax.all_to_all(slot_losses.reshape(layout), "rel", split_axis=0, concat_axis=0, tiled=True),
    )
    head_grad = from_buckets(back_grads, position)
    losses = from_buckets(back_losses, position)
    summed = lax.psum(partial_value.astype(jnp.bfloat16), "grp").astype(jnp.float32)
    new_rel, new_accum = adagrad_rows(rel_weight, rel_accum, summed)
    return (losses, head_grad, new_rel, new_accum)


def per_device(head_ids, relations, tail_ids, neg_owner, entities, rel_weight, rel_accum):
    rows_here = head_ids.shape[0]
    width = entities.shape[1]
    shard_rows = entities.shape[0]
    owner_count = lax.axis_size("rel")
    local_rels = rel_weight.shape[0]
    rel_count = owner_count * local_rels
    capacity = 2 * rows_here // rel_count
    slots = rel_count * capacity
    half = local_rels // 2
    core = lax.axis_index("core")
    mine = lax.dynamic_slice_in_dim(rel_weight, core * half, half, 0).astype(BF)
    matrices = lax.all_gather(mine, "rel", axis=0, tiled=False)
    matrices = lax.all_gather(matrices, "core", axis=1, tiled=False)
    matrices = matrices.reshape(rel_count, width, width)
    negatives = broadcast(entities, ("x", "core", "rel"), neg_owner[0])
    rel_ids = relations[:, 0]
    rel_hot = one_hot(rel_ids, rel_count)
    order = jnp.arange(rows_here, dtype=jnp.int32)
    lower = (order[:, None] >= order[None, :]).astype(BF)
    running = jnp.dot(lower, rel_hot, preferred_element_type=F32)
    rank = jnp.sum(running * rel_hot.astype(F32), axis=-1).astype(jnp.int32) - 1
    position = rel_ids * capacity + rank
    bucket = (jnp.arange(slots, dtype=jnp.int32)[:, None] == position[None, :]).astype(BF)
    head_rows = select_rows(one_hot(head_ids, shard_rows), entities)
    tail_rows = select_rows(one_hot(tail_ids, shard_rows), entities)
    held_rows = select_rows(bucket, head_rows).reshape(rel_count, capacity, width)
    projected = jnp.einsum("rcd,rde->rce", held_rows, matrices, preferred_element_type=F32).astype(
        BF
    )
    query_rows = select_back(bucket, projected.reshape(slots, width))
    losses, grad_query = score_rows(query_rows, tail_rows, negatives)
    grad_rows = select_rows(bucket, grad_query).reshape(rel_count, capacity, width)
    partial_value = jnp.einsum(
        "rcd,rce->rde", held_rows, grad_rows, preferred_element_type=F32
    ).astype(BF)
    partial_value = partial_value.reshape(owner_count, 2, half, width, width)
    summed = lax.psum_scatter(partial_value, "core", scatter_dimension=1, tiled=True)
    summed = lax.psum_scatter(summed, "rel", scatter_dimension=0, tiled=True)
    summed = lax.psum(summed.reshape(half, width, width), "x")
    summed = lax.all_gather(summed, "core", axis=0, tiled=True).astype(F32)
    head_back = jnp.einsum("rce,rde->rcd", grad_rows, matrices, preferred_element_type=F32).astype(
        BF
    )
    head_grad = select_back(bucket, head_back.reshape(slots, width))
    new_rel, new_accum = adagrad(rel_weight, rel_accum, summed)
    return (losses, head_grad, new_rel, new_accum)


GATHER_LIMIT = 16 * 1024 * 1024


def solution(mesh):
    placed = (
        P(("grp", "rel")),
        P(("grp", "rel"), None),
        P(("grp", "rel")),
        P(),
        P(("grp", "rel"), None),
        P("rel", None, None),
        P("rel", None),
    )
    outs = (P(("grp", "rel")), P(("grp", "rel"), None), P("rel", None, None), P("rel", None))
    rows_step = jax.shard_map(
        per_device_rows, mesh=mesh, in_specs=placed, out_specs=outs, check_vma=False
    )
    groups, owners = mesh.devices.shape
    split = jax.sharding.Mesh(mesh.devices.reshape(groups // 2, 2, owners), ("x", "core", "rel"))

    def respec(spec):
        return P(*[("x", "core", "rel") if part == ("grp", "rel") else part for part in spec])

    local_step = jax.shard_map(
        per_device,
        mesh=split,
        in_specs=tuple((respec(s) for s in placed)),
        out_specs=tuple((respec(s) for s in outs)),
        check_vma=False,
    )

    def step(head_ids, relations, tail_ids, neg_owner, entities, rel_weight, rel_accum):
        args = (head_ids, relations, tail_ids, neg_owner, entities, rel_weight, rel_accum)
        width = rel_weight.shape[-1]
        if rel_weight.shape[0] * width * width * 2 <= GATHER_LIMIT:
            return local_step(*args)
        return rows_step(*args)

    return step
```

profile of v0, /device:TPU:0, one launch (start us, length us, event | category | flops | bytes accessed | tf_op | source)
XLA Modules:
  0.0 616.2 jit_solution(17975725279980683553)
XLA Ops:
  8.0 2.7 dynamic-slice_convert_fusion
  10.8 127.9 %all-gather.8.cloned.1.call-done = bf16[16,512,512]{2,1,0:T(8,128)(2,1)} async-done(((bf16[2,512,512]{2,1,0:T(8,128)(2,1)}), bf16[16,512,512]{2,1,0:T(8,128)(2,1)}) %all-gather.8.cloned.1.call-update) | async-done | bytes 8388624 | tf_op jit(solution)/shard_map/all_gather | solution.py:141
  138.8 0.0 all-reduce.5.cloned.1.call-start
  139.5 0.4 copy-done
  140.0 1.1 broadcast_select_fusion
  141.1 0.0 all-reduce.9.cloned.1.call-start
  141.1 1.5 fusion.27
  142.7 2.6 fusion.62
  145.3 10.4 %fusion.12 = bf16[4096,512]{1,0:T(8,128)(2,1)} fusion(s32[2048]{0:T(1024)S(1)} %add_add_fusion, bf16[2048,512]{1,0:T(8,128)(2,1)S(1)} %fusion.62), kind=kOutput, calls=%fused_computation.19 | convolution fusion | flops 8600420352 | bytes 6299648 | tf_op jit(solution)/shard_map/dot_general | solution.py:21
  155.7 12.9 %all-gather.10.cloned.1.call-done = bf16[8,4,512,512]{3,2,1,0:T(8,128)(2,1)} async-done(((bf16[8,2,512,512]{3,2,1,0:T(8,128)(2,1)}), bf16[8,4,512,512]{3,2,1,0:T(8,128)(2,1)}) %all-gather.10.cloned.1.call-update) | async-done | bytes 16777232 | tf_op jit(solution)/shard_map/all_gather | solution.py:142
  168.6 9.5 %convolution_convert_fusion.2 = bf16[32,128,512]{2,1,0:T(8,128)(2,1)S(1)} fusion(bf16[32,128,512]{2,1,0:T(8,128)(2,1)} %bitcast.50, bf16[32,512,512]{2,1,0:T(8,128)(2,1)} %bitcast.45), kind=kOutput, calls=%fused_computation.38 | convolution fusion | flops 2149580800 | bytes 25165824 | tf_op jit(solution)/shard_map/rcd,rde->rce/dot_general | solution.py:156
  178.1 9.4 %fusion.22 = bf16[2048,512]{0,1:T(8,128)(2,1)S(1)} fusion(bf16[4096,512]{1,0:T(8,128)(2,1)S(1)} %bitcast.53, s32[2048]{0:T(1024)S(1)} %add_add_fusion), kind=kOutput, calls=%fused_computation.33 | convolution fusion | flops 8599371776 | bytes 6299648 | tf_op jit(solution)/shard_map/dot_general | solution.py:25
  187.5 1.4 copy-done.7
  188.8 4.3 fusion.14
  193.2 88.0 %all-reduce.5.cloned.1.call-done = bf16[1024,512]{1,0:T(8,128)(2,1)} async-done(((bf16[1024,512]{1,0:T(8,128)(2,1)}), bf16[1024,512]{1,0:T(8,128)(2,1)}) %all-reduce.5.cloned.1.call-update) | async-done | bytes 1048592 | tf_op jit(solution)/shard_map/psum | solution.py:13
  281.2 10.7 %fusion.9 = (f32[2048]{0:T(1024)S(1)}, f32[2048,1024]{0,1:T(8,128)}) fusion(bf16[1024,512]{1,0:T(8,128)(2,1)} %all-reduce.5.cloned.1.call-done, bf16[2048,512]{0,1:T(8,128)(2,1)} %copy-done.7), kind=kOutput, calls=%fused_computation.13 | convolution fusion | flops 2162161664 | bytes 11542528 | tf_op jit(solution)/shard_map/dot_general | solution.py:32
  291.9 0.6 divide_negate_fusion
  292.5 20.4 %fusion.13 = bf16[4096,512]{1,0:T(8,128)(2,1)} fusion(s32[2048]{0:T(1024)S(1)} %add_add_fusion, bf16[2048,512]{0,1:T(8,128)(2,1)} %get-tuple-element.9, bf16[1024,512]{1,0:T(8,128)(2,1)S(1)} %copy-done.3, f32[2048,1024]{0,1:T(8,128)} %get-tuple-element.11, f32[2048]{0:T(1024)S(1)} %get-tuple-element.6), kind=kOutput, calls=%fused_computation.20 | convolution fusion | flops 10762584064 | bytes 15745024 | tf_op jit(solution)/shard_map/dot_general | solution.py:21
  312.9 10.9 %convolution_convert_fusion = bf16[32,512,512]{2,1,0:T(8,128)(2,1)} fusion(bf16[32,128,512]{2,1,0:T(8,128)(2,1)} %bitcast.51, bf16[32,128,512]{2,1,0:T(8,128)(2,1)} %bitcast.48), kind=kOutput, calls=%fused_computation.12 | convolution fusion | flops 2155872256 | bytes 25165824 | tf_op jit(solution)/shard_map/rcd,rce->rde/dot_general | solution.py:162
  323.8 0.0 reduce-scatter.5.cloned.1.call-start
  323.9 0.6 copy-done.6
  324.5 0.6 dynamic-slice
  325.1 58.9 %all-reduce.9.cloned.1.call-done = bf16[8,2,2,512,512]{4,3,2,1,0:T(8,128)(2,1)} async-done(((bf16[8,2,2,512,512]{4,3,2,1,0:T(8,128)(2,1)}), bf16[8,2,2,512,512]{4,3,2,1,0:T(8,128)(2,1)}) %all-reduce.9.cloned.1.call-update) | async-done | bytes 16777232
  384.0 8.0 %constant_dynamic-slice_fusion = bf16[8,1,2,512,512]{4,3,2,1,0:T(8,128)(2,1)} fusion(bf16[8,2,2,512,512]{4,3,2,1,0:T(8,128)(2,1)} %all-reduce.9.cloned.1.call-done, u32[]{:T(128)} %bitcast.16), kind=kLoop, calls=%fused_computation.52 | loop fusion | bytes 16777220
  392.0 0.0 all-reduce.7.cloned.1.call-start
  392.0 148.8 %reduce-scatter.5.cloned.1.call-done = bf16[1,1,2,512,512]{4,3,2,1,0:T(8,128)(2,1)} async-done(((bf16[8,1,2,512,512]{4,3,2,1,0:T(8,128)(2,1)}), bf16[1,1,2,512,512]{4,3,2,1,0:T(8,128)(2,1)}) %reduce-scatter.5.cloned.1.call-update) | async-done | bytes 1048592 | tf_op jit(solution)/shard_map/reduce_scatter | solution.py:167
  540.9 39.1 %all-reduce.7.cloned.1.call-done = bf16[2,512,512]{2,1,0:T(8,128)(2,1)} async-done(((bf16[2,512,512]{2,1,0:T(8,128)(2,1)}), bf16[2,512,512]{2,1,0:T(8,128)(2,1)}) %all-reduce.7.cloned.1.call-update) | async-done | bytes 1048592 | tf_op jit(solution)/shard_map/psum | solution.py:168
  580.0 10.6 %convolution_convert_fusion.1 = bf16[32,128,512]{2,1,0:T(8,128)(2,1)S(1)} fusion(bf16[32,128,512]{2,1,0:T(8,128)(2,1)} %bitcast.49, bf16[32,512,512]{2,1,0:T(8,128)(2,1)} %bitcast.46), kind=kOutput, calls=%fused_computation.37 | convolution fusion | flops 2149580800 | bytes 25165824 | tf_op jit(solution)/shard_map/rce,rde->rcd/dot_general | solution.py:170
  590.6 10.1 %fusion.23 = bf16[2048,512]{1,0:T(8,128)(2,1)} fusion(bf16[4096,512]{1,0:T(8,128)(2,1)S(1)} %bitcast.52, s32[2048]{0:T(1024)S(1)} %add_add_fusion), kind=kOutput, calls=%fused_computation.34 | convolution fusion | flops 8599371776 | bytes 6299648 | tf_op jit(solution)/shard_map/dot_general | solution.py:25
  600.7 2.1 fusion.17
  602.8 0.6 fusion.36
  603.4 5.5 fusion.18
  (25 shorter events, 0.3 us)
Async XLA Ops:
  8.0 130.7 %all-gather.8.cloned.1.call-start = ((), (), s32[]{:S(2)}) async-start(), calls=%async_computation.5 | async-start | bytes 9437184 | tf_op jit(solution)/shard_map/all_gather | solution.py:141
  10.8 157.8 %all-gather.10.cloned.1.call-start = ((), (), s32[]{:S(2)}) async-start(), calls=%async_computation.6 | async-start | bytes 25165824 | tf_op jit(solution)/shard_map/all_gather | solution.py:142
  138.7 1.2 copy-start
  138.7 2.4 copy-start.1
  138.8 142.4 %all-reduce.5.cloned.1.call-start = ((), (), s32[]{:S(2)}) async-start(), calls=%async_computation.1 | async-start | bytes 2097152 | tf_op jit(solution)/shard_map/psum | solution.py:13
  141.1 1.6 copy-start.4
  141.1 242.9 %all-reduce.9.cloned.1.call-start = ((), (), s32[]{:S(2)}) async-start(), calls=%async_computation.7 | async-start | bytes 33554432
  178.1 10.8 %copy-start.5 = (s32[2048]{0:T(1024)S(1)}, s32[2048]{0:T(1024)}, u32[]{:S(2)}) copy-start(s32[2048]{0:T(1024)} %param.9) | copy-start | bytes 24580
  187.5 1.4 copy-start.7
  281.2 11.3 %copy-start.3 = (bf16[1024,512]{1,0:T(8,128)(2,1)S(1)}, bf16[1024,512]{1,0:T(8,128)(2,1)}, u32[]{:S(2)}) copy-start(bf16[1024,512]{1,0:T(8,128)(2,1)} %all-reduce.5.cloned.1.call-done) | copy-start | bytes 3145732
  323.8 0.7 copy-start.6
  323.8 216.9 %reduce-scatter.5.cloned.1.call-start = ((), (), s32[]{:S(2)}) async-start(), calls=%async_computation.2 | async-start | bytes 9437184 | tf_op jit(solution)/shard_map/reduce_scatter | solution.py:167
  392.0 188.0 %all-reduce.7.cloned.1.call-start = ((), (), s32[]{:S(2)}) async-start(), calls=%async_computation.3 | async-start | bytes 2097152 | tf_op jit(solution)/shard_map/psum | solution.py:168
  540.8 59.9 %all-gather.6.cloned.1.call-start = ((), (), s32[]{:S(2)}) async-start(), calls=%async_computation.4 | async-start | bytes 3145728 | tf_op jit(solution)/shard_map/all_gather | solution.py:169
  590.6 12.2 %copy-start.2 = (f32[4,512]{1,0:T(4,128)S(1)}, f32[4,512]{1,0:T(4,128)}, u32[]{:S(2)}) copy-start(f32[4,512]{1,0:T(4,128)} %param.13) | copy-start | bytes 24580
Sparse Core Ops, SparseCore 0:
  11.5 127.1 all-gather.7
  140.3 28.2 all-gather.9
  324.0 59.9 all-reduce.8
  392.1 148.6 reduce-scatter.4
  580.1 10.5 all-gather.5
Sparse Core Ops, SparseCore 1:
  144.4 136.7 all-reduce.4
  540.9 39.0 all-reduce.6
where the time goes:
time: 626 us; the launch traced here: 616 us
  waiting for transfers between devices  476 us (76%)
  matrix products  100 us (16%)
  between operations  16.3 us (3%)
  local copies, waits for them, and re-layouts  13.6 us (2%)
  other arithmetic  9.88 us (2%)
    reduce_scatter x1, waiting for transfers between devices, per_device(): summed = lax.psum_scatter(summed, 'rel', scatter_dimension=0, tiled=True)  149 us
    all_gather x1, waiting for transfers between devices, per_device(): matrices = lax.all_gather(mine, 'rel', axis=0, tiled=False)  128 us
    psum x1, waiting for transfers between devices, broadcast(): return lax.psum(jnp.where(mine, shard, jnp.zeros_like(shard)), axis)  88 us
    unnamed x8, waiting for transfers between devices  59 us
    psum x1, waiting for transfers between devices, per_device(): summed = lax.psum(summed.reshape(half, width, width), 'x')  39.1 us
    dot_general x4, matrix products, select_rows(): return jnp.dot(selector, rows, preferred_element_type=F32).astype(BF)  37.7 us
    dot_general x2, matrix products, select_back(): lax.dot_general(selector, rows, (((0,), (0,)), ((), ())), preferred_eleme...  19.4 us
    all_gather x1, waiting for transfers between devices, per_device(): matrices = lax.all_gather(matrices, 'core', axis=1, tiled=False)  12.9 us
  transfers between devices with their start and end apart: 7, of which 6 were waited for; matrix products, arithmetic and copies ran while one was open for 10% of the time, Pallas kernels for 0%

commit v1 on v0

--- a/solution.py
+++ b/solution.py
@@ -10,7 +10,7 @@
 
 def broadcast(shard, axis, root):
     mine = lax.axis_index(axis) == root
-    return lax.psum(jnp.where(mine, shard, jnp.zeros_like(shard)), axis)
+    return jnp.sum(lax.all_gather(jnp.where(mine, shard, jnp.zeros_like(shard)), axis), axis=0)
 
 
 def one_hot(ids, count):

time: 626 us -> 723 us (1.15)
  waiting for transfers between devices: 476 us -> 563 us
  other arithmetic: 9.88 us -> 21.3 us
    all_gather x0 -> x1, waiting for transfers between devices: none -> 174 us  [broadcast(): lax.all_gather(jnp.where(mine, shard, jnp.zeros_like(shard)), axis)]
    psum x1 -> x0, waiting for transfers between devices: 88 us -> none  [broadcast(): return lax.psum(jnp.where(mine, shard, jnp.zeros_like(shard)), axis)]
    reduce_sum x0 -> x1, other arithmetic: none -> 11.4 us  [broadcast(): jnp.sum(lax.all_gather(jnp.where(mine, shard, jnp.zeros_like(shard)), axi...]
  transfers between devices with their start and end apart: 7 -> 7, of which waited for: 6 -> 6; matrix products, arithmetic and copies ran while one was open for 10% -> 8% of each run, Pallas kernels for 0% -> 0%
where the time goes in v1:
time: 723 us; the launch traced here: 713 us
  waiting for transfers between devices  563 us (78%)
  matrix products  100 us (14%)
  other arithmetic  21.3 us (3%)
  between operations  15.2 us (2%)
  local copies, waits for them, and re-layouts  13.7 us (2%)
    all_gather x1, waiting for transfers between devices, broadcast(): lax.all_gather(jnp.where(mine, shard, jnp.zeros_like(shard)), axis)  174 us
    reduce_scatter x1, waiting for transfers between devices, per_device(): summed = lax.psum_scatter(summed, 'rel', scatter_dimension=0, tiled=True)  149 us
    all_gather x1, waiting for transfers between devices, per_device(): matrices = lax.all_gather(mine, 'rel', axis=0, tiled=False)  128 us
    unnamed x8, waiting for transfers between devices  58.1 us
    psum x1, waiting for transfers between devices, per_device(): summed = lax.psum(summed.reshape(half, width, width), 'x')  41.3 us
    dot_general x4, matrix products, select_rows(): return jnp.dot(selector, rows, preferred_element_type=F32).astype(BF)  37.7 us
    dot_general x2, matrix products, select_back(): lax.dot_general(selector, rows, (((0,), (0,)), ((), ())), preferred_eleme...  19.5 us
  transfers between devices with their start and end apart: 7, of which 6 were waited for; matrix products, arithmetic and copies ran while one was open for 8% of the time, Pallas kernels for 0%

profile of v1, /device:TPU:0, one launch (start us, length us, event | category | flops | bytes accessed | tf_op | source)
XLA Modules:
  0.0 713.4 jit_solution(14232001534751616271)
XLA Ops:
  7.2 2.7 dynamic-slice_convert_fusion
  10.0 127.9 %all-gather.10.cloned.1.call-done = bf16[16,512,512]{2,1,0:T(8,128)(2,1)} async-done(((bf16[2,512,512]{2,1,0:T(8,128)(2,1)}), bf16[16,512,512]{2,1,0:T(8,128)(2,1)}) %all-gather.10.cloned.1.call-update) | async-done | bytes 8388624 | tf_op jit(solution)/shard_map/all_gather | solution.py:141
  138.7 0.4 copy-done
  139.1 1.0 broadcast_select_fusion
  140.2 0.0 all-reduce.6.cloned.1.call-start
  140.3 1.5 fusion.27
  141.8 2.6 fusion.62
  144.4 10.4 %fusion.12 = bf16[4096,512]{1,0:T(8,128)(2,1)} fusion(s32[2048]{0:T(1024)S(1)} %add_add_fusion, bf16[2048,512]{1,0:T(8,128)(2,1)S(1)} %fusion.62), kind=kOutput, calls=%fused_computation.19 | convolution fusion | flops 8600420352 | bytes 6299648 | tf_op jit(solution)/shard_map/dot_general | solution.py:21
  154.8 13.0 %all-gather.12.cloned.1.call-done = bf16[8,4,512,512]{3,2,1,0:T(8,128)(2,1)} async-done(((bf16[8,2,512,512]{3,2,1,0:T(8,128)(2,1)}), bf16[8,4,512,512]{3,2,1,0:T(8,128)(2,1)}) %all-gather.12.cloned.1.call-update) | async-done | bytes 16777232 | tf_op jit(solution)/shard_map/all_gather | solution.py:142
  167.7 9.4 %convolution_convert_fusion.2 = bf16[32,128,512]{2,1,0:T(8,128)(2,1)S(1)} fusion(bf16[32,128,512]{2,1,0:T(8,128)(2,1)} %bitcast.51, bf16[32,512,512]{2,1,0:T(8,128)(2,1)} %bitcast.46), kind=kOutput, calls=%fused_computation.38 | convolution fusion | flops 2149580800 | bytes 25165824 | tf_op jit(solution)/shard_map/rcd,rde->rce/dot_general | solution.py:156
  177.2 9.4 %fusion.22 = bf16[2048,512]{0,1:T(8,128)(2,1)S(1)} fusion(bf16[4096,512]{1,0:T(8,128)(2,1)S(1)} %bitcast.55, s32[2048]{0:T(1024)S(1)} %add_add_fusion), kind=kOutput, calls=%fused_computation.33 | convolution fusion | flops 8599371776 | bytes 6299648 | tf_op jit(solution)/shard_map/dot_general | solution.py:25
  186.6 1.3 copy-done.6
  187.9 4.3 fusion.14
  192.3 173.9 %all-gather.14.cloned.1.call-done = bf16[32768,512]{1,0:T(8,128)(2,1)} async-done(((bf16[1024,512]{1,0:T(8,128)(2,1)}), bf16[32768,512]{1,0:T(8,128)(2,1)}) %all-gather.14.cloned.1.call-update) | async-done | bytes 33554448 | tf_op jit(solution)/shard_map/all_gather | solution.py:13
  366.1 11.4 %reduce_sum.50 = bf16[1024,512]{1,0:T(8,128)(2,1)S(1)} reduce(bf16[32,1024,512]{2,1,0:T(8,128)(2,1)} %bitcast.53, bf16[]{:T(256)} %constant.44.clone.1), dimensions={0}, to_apply=%region_2.3 | reduce | flops 16252928 | bytes 34603008 | tf_op jit(solution)/shard_map/reduce_sum | solution.py:13
  377.6 10.3 %fusion.9 = (f32[2048]{0:T(1024)S(1)}, f32[2048,1024]{0,1:T(8,128)}) fusion(bf16[1024,512]{1,0:T(8,128)(2,1)S(1)} %reduce_sum.50, bf16[2048,512]{0,1:T(8,128)(2,1)} %copy-done.6), kind=kOutput, calls=%fused_computation.13 | convolution fusion | flops 2162161664 | bytes 11542528 | tf_op jit(solution)/shard_map/dot_general | solution.py:32
  387.9 0.6 divide_negate_fusion
  388.5 20.4 %fusion.13 = bf16[4096,512]{1,0:T(8,128)(2,1)} fusion(s32[2048]{0:T(1024)S(1)} %add_add_fusion, bf16[2048,512]{0,1:T(8,128)(2,1)} %get-tuple-element.9, bf16[1024,512]{1,0:T(8,128)(2,1)S(1)} %reduce_sum.50, f32[2048,1024]{0,1:T(8,128)} %get-tuple-element.11, f32[2048]{0:T(1024)S(1)} %get-tuple-element.6), kind=kOutput, calls=%fused_computation.20 | convolution fusion | flops 10762584064 | bytes 15745024 | tf_op jit(solution)/shard_map/dot_general | solution.py:21
  408.9 11.0 %convolution_convert_fusion = bf16[32,512,512]{2,1,0:T(8,128)(2,1)} fusion(bf16[32,128,512]{2,1,0:T(8,128)(2,1)} %bitcast.52, bf16[32,128,512]{2,1,0:T(8,128)(2,1)} %bitcast.49), kind=kOutput, calls=%fused_computation.12 | convolution fusion | flops 2155872256 | bytes 25165824 | tf_op jit(solution)/shard_map/rcd,rce->rde/dot_general | solution.py:162
  419.9 0.0 reduce-scatter.5.cloned.1.call-start
  420.0 0.6 copy-done.5
  420.6 0.6 dynamic-slice
  421.2 58.0 %all-reduce.6.cloned.1.call-done = bf16[8,2,2,512,512]{4,3,2,1,0:T(8,128)(2,1)} async-done(((bf16[8,2,2,512,512]{4,3,2,1,0:T(8,128)(2,1)}), bf16[8,2,2,512,512]{4,3,2,1,0:T(8,128)(2,1)}) %all-reduce.6.cloned.1.call-update) | async-done | bytes 16777232
  479.2 8.0 %constant_dynamic-slice_fusion = bf16[8,1,2,512,512]{4,3,2,1,0:T(8,128)(2,1)} fusion(bf16[8,2,2,512,512]{4,3,2,1,0:T(8,128)(2,1)} %all-reduce.6.cloned.1.call-done, u32[]{:T(128)} %bitcast.17), kind=kLoop, calls=%fused_computation.52 | loop fusion | bytes 16777220
  487.2 0.0 all-reduce.4.cloned.1.call-start
  487.2 148.8 %reduce-scatter.5.cloned.1.call-done = bf16[1,1,2,512,512]{4,3,2,1,0:T(8,128)(2,1)} async-done(((bf16[8,1,2,512,512]{4,3,2,1,0:T(8,128)(2,1)}), bf16[1,1,2,512,512]{4,3,2,1,0:T(8,128)(2,1)}) %reduce-scatter.5.cloned.1.call-update) | async-done | bytes 1048592 | tf_op jit(solution)/shard_map/reduce_scatter | solution.py:167
  636.1 41.3 %all-reduce.4.cloned.1.call-done = bf16[2,512,512]{2,1,0:T(8,128)(2,1)} async-done(((bf16[2,512,512]{2,1,0:T(8,128)(2,1)}), bf16[2,512,512]{2,1,0:T(8,128)(2,1)}) %all-reduce.4.cloned.1.call-update) | async-done | bytes 1048592 | tf_op jit(solution)/shard_map/psum | solution.py:168
  677.4 10.6 %convolution_convert_fusion.1 = bf16[32,128,512]{2,1,0:T(8,128)(2,1)S(1)} fusion(bf16[32,128,512]{2,1,0:T(8,128)(2,1)} %bitcast.50, bf16[32,512,512]{2,1,0:T(8,128)(2,1)} %bitcast.47), kind=kOutput, calls=%fused_computation.37 | convolution fusion | flops 2149580800 | bytes 25165824 | tf_op jit(solution)/shard_map/rce,rde->rcd/dot_general | solution.py:170
  688.0 10.1 %fusion.23 = bf16[2048,512]{1,0:T(8,128)(2,1)} fusion(bf16[4096,512]{1,0:T(8,128)(2,1)S(1)} %bitcast.54, s32[2048]{0:T(1024)S(1)} %add_add_fusion), kind=kOutput, calls=%fused_computation.34 | convolution fusion | flops 8599371776 | bytes 6299648 | tf_op jit(solution)/shard_map/dot_general | solution.py:25
  698.1 2.1 fusion.17
  700.2 0.6 fusion.36
  700.8 5.5 fusion.18
  (24 shorter events, 0.3 us)
Async XLA Ops:
  7.2 130.7 %all-gather.10.cloned.1.call-start = ((), (), s32[]{:S(2)}) async-start(), calls=%async_computation.4 | async-start | bytes 9437184 | tf_op jit(solution)/shard_map/all_gather | solution.py:141
  9.9 157.8 %all-gather.12.cloned.1.call-start = ((), (), s32[]{:S(2)}) async-start(), calls=%async_computation.5 | async-start | bytes 25165824 | tf_op jit(solution)/shard_map/all_gather | solution.py:142
  137.9 1.2 copy-start
  137.9 2.4 copy-start.1
  137.9 228.2 %all-gather.14.cloned.1.call-start = ((), (), s32[]{:S(2)}) async-start(), calls=%async_computation.6 | async-start | bytes 34603008 | tf_op jit(solution)/shard_map/all_gather | solution.py:13
  140.2 1.6 copy-start.3
  140.2 338.9 %all-reduce.6.cloned.1.call-start = ((), (), s32[]{:S(2)}) async-start(), calls=%async_computation.7 | async-start | bytes 33554432
  177.1 10.8 %copy-start.4 = (s32[2048]{0:T(1024)S(1)}, s32[2048]{0:T(1024)}, u32[]{:S(2)}) copy-start(s32[2048]{0:T(1024)} %param.9) | copy-start | bytes 24580
  186.6 1.4 copy-start.6
  419.9 0.7 copy-start.5
  419.9 216.1 %reduce-scatter.5.cloned.1.call-start = ((), (), s32[]{:S(2)}) async-start(), calls=%async_computation.1 | async-start | bytes 9437184 | tf_op jit(solution)/shard_map/reduce_scatter | solution.py:167
  487.2 190.2 %all-reduce.4.cloned.1.call-start = ((), (), s32[]{:S(2)}) async-start(), calls=%async_computation.2 | async-start | bytes 2097152 | tf_op jit(solution)/shard_map/psum | solution.py:168
  636.0 62.1 %all-gather.8.cloned.1.call-start = ((), (), s32[]{:S(2)}) async-start(), calls=%async_computation.3 | async-start | bytes 3145728 | tf_op jit(solution)/shard_map/all_gather | solution.py:169
  688.0 12.2 %copy-start.2 = (f32[4,512]{1,0:T(4,128)S(1)}, f32[4,512]{1,0:T(4,128)}, u32[]{:S(2)}) copy-start(f32[4,512]{1,0:T(4,128)} %param.13) | copy-start | bytes 24580
Sparse Core Ops, SparseCore 0:
  10.7 127.1 all-gather.9
  139.5 28.2 all-gather.11
  170.7 195.3 all-gather.13
  420.1 59.0 all-reduce.5
  487.3 148.6 reduce-scatter.4
  638.1 39.2 all-reduce.3
  678.9 10.5 all-gather.7
